TPU v7x, 256 devices: a whole 4x4x8 slice. The times are simulated.
256 devices in a mesh: group: 16 (over y, x), dp: 8 (over z), space: 2 (over core).
Axes of the slice: x: 4, y: 4, z: 8, core: 2. Of those that a mesh axis runs over, the one named last changes fastest.
Arguments:
- video: bfloat16 [8, 32, 16, 64, 256], P('dp', 'group', 'space'), may hold values from -6 to 6
- cotangent: bfloat16 [8, 32, 16, 64, 256], P('dp', 'group', 'space'), may hold values from -6 to 6
- weight: bfloat16 [6912, 256], replicated, may hold values from -0.078125 to 0.078125
- clip_id: int32 [8, 32], P('dp', 'group'), may hold values from 0 to 3, never falling along the last dimension, each value on 1 to 16 neighbouring positions
Outputs:
- activation: bfloat16 [8, 32, 16, 64, 256], P('dp', 'group', 'space')
- grad_video: bfloat16 [8, 32, 16, 64, 256], P('dp', 'group', 'space')
- grad_weight: float32 [27, 65536], P(None, ('group', 'dp', 'space'))
Inputs may be any that keep to these rules, and one draw needn't show every extreme that they name: `clip_id`: clip numbers never fall along a stream's frames; every clip spans at most 16 frames and one spans exactly that many.
All inputs are finite; a program needn't handle non-finite values.
Results may differ from a plain program's by a relative error of at most 0.0053.
Values may be sent and summed in bfloat16 or wider, within the bound.
No kernel may reach another device: no remote copies, remote signals or barrier semaphores. Data moves between devices by JAX's collectives and lax.ppermute only.
A program may use at most 128 MiB of HBM per device.

v0:
```python
import jax
import jax.numpy as jnp
from jax import lax
from jax.sharding import PartitionSpec as P


def entering(value, axis, join, neutral):
    count, mine = (lax.axis_size(axis), lax.axis_index(axis))
    pieces = jax.tree.map(lambda part: lax.all_gather(part, axis), value)
    total = jax.tree.map(
        lambda part, zero: jnp.full_like(part, 0) + jnp.asarray(zero, part.dtype), value, neutral
    )

    def lap(position, total):
        longer = join(total, jax.tree.map(lambda part: part[position], pieces))
        return jax.tree.map(lambda new, old: jnp.where(position < mine, new, old), longer, total)

    return lax.fori_loop(0, count - 1, lap, total)


def passed_along(value, axis, by):
    length = lax.axis_size(axis)
    pairs = [(i, i + by) for i in range(length) if 0 <= i + by < length]
    return lax.ppermute(value, axis, pairs)


def with_halo(block, sides, width):
    for axis, dim in sides:
        count = lax.axis_size(axis)
        forward = [(i, i + 1) for i in range(count - 1)]
        backward = [(target, source) for source, target in forward]
        low = lax.ppermute(
            lax.slice_in_dim(block, block.shape[dim] - width, None, axis=dim), axis, forward
        )
        high = lax.ppermute(lax.slice_in_dim(block, 0, width, axis=dim), axis, backward)
        block = jnp.concatenate([low, block, high], axis=dim)
    return block


def merge_summary(earlier, later):
    early_last, early_tail, early_count = earlier
    late_last, late_tail, late_count = later
    last_clip = jnp.where(late_count > 0, late_last, early_last)
    joined = (late_tail == late_count) & (early_last == late_last)
    tail_len = jnp.where(late_count > 0, late_tail + jnp.where(joined, early_tail, 0), early_tail)
    return (last_clip, tail_len, early_count + late_count)


def local(video, cotangent, weight, clip_id):
    frames = video.shape[1]
    rows = video.shape[2]
    cols = video.shape[3]
    chans = video.shape[4]
    last_clip = clip_id[:, -1]
    tail_len = jnp.sum((clip_id == last_clip[:, None]).astype(jnp.int32), axis=1)
    counted = jnp.full_like(last_clip, frames)
    identity = (jnp.full_like(last_clip, -1), jnp.zeros_like(last_clip), jnp.zeros_like(last_clip))
    before = entering((last_clip, tail_len, counted), "group", merge_summary, identity)
    prev_last = before[0]
    prev_tail = before[1]
    older = jnp.where(prev_tail >= 2, prev_last, -2)
    extended = jnp.concatenate([older[:, None], prev_last[:, None], clip_id], axis=1)
    boundary = clip_id != extended[:, 1:-1]
    index = jnp.arange(frames, dtype=jnp.int32)[None, :]
    start = lax.cummax(jnp.where(boundary, index, 0), axis=1)
    carried = (clip_id == prev_last[:, None]) & (start == 0) & jnp.logical_not(boundary[:, :1])
    position = index - start + jnp.where(carried, prev_tail[:, None], 0)
    masks = jnp.stack([extended[:, 2 - k : 2 - k + frames] == clip_id for k in range(3)], axis=0)
    maskf = masks.astype(jnp.float32)
    omega = 0.37 * (jnp.arange(chans) % 8 + 1).astype(jnp.float32)
    embed = jnp.sin(position.astype(jnp.float32)[:, :, None] * omega)
    shifted = (video.astype(jnp.float32) + embed[:, :, None, None, :]).astype(jnp.bfloat16)
    past = passed_along(shifted, "group", 1)
    widened = jnp.concatenate([past, shifted], axis=1)
    widened = with_halo(widened, (("space", 2),), 1)
    widened = jnp.pad(widened, ((0, 0), (0, 0), (0, 0), (1, 1), (0, 0)))
    stacked = jnp.concatenate([widened[:, :, :, b : b + cols] for b in range(3)], axis=4)
    taps = weight.reshape(3, 3, 3 * chans, chans)
    pre = jnp.zeros(video.shape, jnp.float32)
    for k in range(3):
        part = jnp.zeros(video.shape, jnp.float32)
        for a in range(3):
            block = stacked[:, 2 - k : 2 - k + frames, a : a + rows]
            part = part + jnp.einsum(
                "sfhwk,kc->sfhwc", block, taps[k, a], preferred_element_type=jnp.float32
            )
        pre = pre + part * maskf[k][:, :, None, None, None]
    sigma = jax.nn.sigmoid(pre)
    activation = (pre * sigma).astype(jnp.bfloat16)
    delta = (cotangent.astype(jnp.float32) * sigma * (1.0 + pre * (1.0 - sigma))).astype(
        jnp.bfloat16
    )
    head_flags = masks.astype(jnp.bfloat16)
    ahead, ahead_flags = passed_along((delta, head_flags), "group", -1)
    gwide = jnp.concatenate([delta, ahead], axis=1)
    flags = jnp.concatenate([maskf, ahead_flags.astype(jnp.float32)], axis=2)
    gwide = with_halo(gwide, (("space", 2),), 1)
    gwide = jnp.pad(gwide, ((0, 0), (0, 0), (0, 0), (1, 1), (0, 0)))
    gstack = jnp.concatenate([gwide[:, :, :, 2 - b : 2 - b + cols] for b in range(3)], axis=4)
    back = (
        weight.reshape(3, 3, 3, chans, chans)
        .transpose(0, 1, 2, 4, 3)
        .reshape(3, 3, 3 * chans, chans)
    )
    grad = jnp.zeros(video.shape, jnp.float32)
    for k in range(3):
        part = jnp.zeros(video.shape, jnp.float32)
        for a in range(3):
            block = gstack[:, k : k + frames, 2 - a : 2 - a + rows]
            part = part + jnp.einsum(
                "sfhwk,kc->sfhwc", block, back[k, a], preferred_element_type=jnp.float32
            )
        grad = grad + part * flags[k][:, k : k + frames, None, None, None]
    terms = []
    for k in range(3):
        masked = delta * masks[k].astype(jnp.bfloat16)[:, :, None, None, None]
        for a in range(3):
            block = stacked[:, 2 - k : 2 - k + frames, a : a + rows]
            terms.append(
                jnp.einsum("sfhwk,sfhwc->kc", block, masked, preferred_element_type=jnp.float32)
            )
    total = jnp.stack(terms).reshape(27, chans * chans)
    reduced = lax.psum_scatter(total, ("group", "dp", "space"), scatter_dimension=1, tiled=True)
    return (activation, grad.astype(jnp.bfloat16), reduced)


def solution(mesh):
    placed = (
        P("dp", "group", "space", None, None),
        P("dp", "group", "space", None, None),
        P(),
        P("dp", "group"),
    )
    return jax.shard_map(
        local,
        mesh=mesh,
        in_specs=placed,
        out_specs=(
            P("dp", "group", "space", None, None),
            P("dp", "group", "space", None, None),
            P(None, ("group", "dp", "space")),
        ),
        check_vma=False,
    )
```

profile of v0, /device:TPU:0, one launch (start us, length us, event | category | flops | bytes accessed | tf_op | source)
XLA Modules:
  0.0 1463.0 jit_solution(13670070295841205196)
XLA Ops:
  7.2 1.2 slice.183
  8.4 1.9 fusion.99
  10.4 1.3 dynamic-slice
  11.6 1.2 bitcast_dynamic-update-slice_fusion
  12.9 1.4 dynamic-update-slice.2
  14.3 0.8 dynamic-update-slice
  15.1 14.8 %all-reduce.5 = (s32[16]{0:T(128)S(1)}, s32[16]{0:T(128)S(1)}, s32[16]{0:T(128)S(1)}) all-reduce(s32[16]{0:T(128)S(1)} %dynamic-update-slice, s32[16]{0:T(128)S(1)} %bitcast_dynamic-update-slice_fusion, s32[16]{0:T(128)S(1)} %dynamic-update-slice.2), channel_id=1, replica_groups=mesh['group'=16,'dp'=8,'space'=2] {'group'}, use_global_device_ids=true, to_apply=%add.2 | all-reduce | flops 48 | bytes 384
  29.9 78.8 %while.15 = (s32[]{:T(128)}, s32[1]{0:T(128)}, s32[1]{0:T(128)}, s32[]{:T(128)}, s32[16,1]{0,1:T(1,128)S(1)}, /*index=5*/s32[16,1]{0,1:T(1,128)S(1)}, s32[16,1]{0,1:T(1,128)S(1)}, s32[]{:T(128)}, s32[1]{0:T(128)}) while((s32[]{:T(128)}, s32[1]{0:T(128)}, s32[1]{0:T(128)}, s32[]{:T(128)}, s32[16,1]{0,1:T(1,128)S(1)}, ...), condition=%wide.region_2.3_spmd, body=%wide.region_1.2_spmd.sunk | while | flops 13 | bytes 249 | solution.py:18
  31.2 0.7 constant_dynamic-slice_fusion.6
  35.1 0.7 constant_dynamic-slice_fusion.5
  36.5 0.7 constant_dynamic-slice_fusion.6
  40.4 0.7 constant_dynamic-slice_fusion.5
  41.8 0.7 constant_dynamic-slice_fusion.6
  47.0 0.7 constant_dynamic-slice_fusion.6
  50.9 0.7 constant_dynamic-slice_fusion.5
  52.3 0.7 constant_dynamic-slice_fusion.6
  57.5 0.7 constant_dynamic-slice_fusion.6
  62.8 0.7 constant_dynamic-slice_fusion.6
  68.0 0.7 constant_dynamic-slice_fusion.6
  71.9 0.7 constant_dynamic-slice_fusion.5
  73.3 0.7 constant_dynamic-slice_fusion.6
  77.2 0.7 constant_dynamic-slice_fusion.5
  78.5 0.7 constant_dynamic-slice_fusion.6
  83.8 0.7 constant_dynamic-slice_fusion.6
  89.0 0.7 constant_dynamic-slice_fusion.6
  94.3 0.7 constant_dynamic-slice_fusion.6
  98.2 0.7 constant_dynamic-slice_fusion.5
  99.5 0.7 constant_dynamic-slice_fusion.6
  104.8 0.7 constant_dynamic-slice_fusion.6
  108.7 0.7 pad_add_fusion.1
  110.3 0.7 convert_bitcast_fusion.2
  111.1 1.1 add_convert_fusion
  112.2 2.5 collective-permute-start
  114.8 0.7 convert_bitcast_fusion.1
  115.6 6.8 collective-permute-done
  122.5 1.3 collective-permute-start.1
  123.8 1.3 collective-permute-start.2
  125.1 1.9 collective-permute-done.2
  127.0 0.8 select_maximum_fusion.3
  127.8 0.9 fusion.103
  129.4 1.4 copy-done
  136.0 2.0 fusion.73
  137.9 1.6 fusion.71
  139.5 1.5 fusion.69
  141.0 1.5 fusion.67
  142.5 1.6 fusion.65
  144.1 1.6 fusion.63
  145.6 1.6 fusion.61
  147.2 1.5 fusion.59
  148.8 1.5 fusion.57
  150.3 1.6 fusion.55
  151.9 7.5 reshape.371
  159.4 1.3 collective-permute-start.6
  160.7 4.3 copy.10
  165.4 1.3 collective-permute-start.3
  166.8 15.7 %collective-permute-done.3 = bf16[1,2,8,64,256]{4,3,2,1,0:T(8,128)(2,1)S(1)} collective-permute-done((bf16[1,2,8,64,256]{4,3,2,1,0:T(8,128)(2,1)}, bf16[1,2,8,64,256]{4,3,2,1,0:T(8,128)(2,1)S(1)}, u32[]{:S(2)}, u32[]{:S(2)}) %collective-permute-start.3) | collective-permute-done | bytes 524320 | tf_op jit(solution)/shard_map/ppermute | solution.py:24
  182.5 0.9 pad_maximum_fusion.3
  183.4 1.6 collective-permute-start.4
  185.0 1.5 collective-permute-start.5
  186.5 2.3 fusion.83
  188.9 1.9 select_maximum_fusion
  190.8 0.9 fusion.102
  196.9 1.4 fusion.72
  198.3 1257.8 %reduce-scatter.2.cloned.1.call-done = f32[27,256]{1,0:T(8,128)} async-done(((f32[27,65536]{1,0:T(8,128)}), f32[27,256]{1,0:T(8,128)}) %reduce-scatter.2.cloned.1.call-update) | async-done | bytes 27664 | tf_op jit(solution)/shard_map/reduce_scatter | solution.py:123
  (57 shorter events, 18.5 us)
Async XLA Ops:
  7.2 1449.0 %reduce-scatter.2.cloned.1.call-start = ((), (), s32[]{:S(2)}) async-start(), calls=%async_computation.1 | async-start | bytes 8421376 | tf_op jit(solution)/shard_map/reduce_scatter | solution.py:123
  112.2 10.2 collective-permute-start
  122.5 2.6 collective-permute-start.1
  123.8 3.2 collective-permute-start.2
  128.7 2.0 copy-start
  134.9 1.0 copy-start.3
  137.9 12.4 copy-start.1
  159.4 5.9 collective-permute-start.6
  165.4 17.1 %collective-permute-start.3 = (bf16[1,2,8,64,256]{4,3,2,1,0:T(8,128)(2,1)}, bf16[1,2,8,64,256]{4,3,2,1,0:T(8,128)(2,1)S(1)}, u32[]{:S(2)}, u32[]{:S(2)}) collective-permute-start(bf16[1,2,8,64,256]{4,3,2,1,0:T(8,128)(2,1)} %copy-done.1), channel_id=1, source_target_pairs={{16,0},{32,16},{48,32},{64,48},{80,64},{96,80},{112,96},{128,112},... | collective-permute-start | bytes 1572872 | tf_op jit(solution)/shard_map/ppermute | solution.py:24
  183.4 5.4 collective-permute-start.4
  185.0 3.8 collective-permute-start.5
  188.8 2.8 copy-start.2
Sparse Core Ops, SparseCore 0:
  159.5 1296.5 reduce-scatter.1
where the time goes:
time: 1460 us
  waiting for transfers between devices  1280 us (88%)
  loops' own time  58.9 us (4%)
  local copies, waits for them, and re-layouts  41.3 us (3%)
  matrix products  26.8 us (2%)
  blocking collectives  14.8 us (1%)
    reduce_scatter x1, waiting for transfers between devices, local(): lax.psum_scatter(total, ('group', 'dp', 'space'), scatter_dimension=1, ti...  1260 us
    another operation x1, loops' own time, entering(): return lax.fori_loop(0, count - 1, lap, total)  58.9 us
  transfers between devices with their start and end apart: 8, of which 5 were waited for; matrix products, arithmetic and copies ran while one was open for 1% of the time, Pallas kernels for 0%

commit v1 on v0

v1 whole, which is shorter than its diff:
```python
import jax
import jax.numpy as jnp
from jax import lax
from jax.sharding import PartitionSpec as P

STAGED = True


def passed_along(value, axis, by):
    length = lax.axis_size(axis)
    pairs = [(i, i + by) for i in range(length) if 0 <= i + by < length]
    return lax.ppermute(value, axis, pairs)


def row_halo(block, axis, dim):
    count = lax.axis_size(axis)
    forward = [(i, i + 1) for i in range(count - 1)]
    backward = [(target, source) for source, target in forward]
    low = lax.ppermute(
        lax.slice_in_dim(block, block.shape[dim] - 1, None, axis=dim), axis, forward
    )
    high = lax.ppermute(lax.slice_in_dim(block, 0, 1, axis=dim), axis, backward)
    return jnp.concatenate([low, block, high], axis=dim)


def clip_tables(clip_id, frames):
    ids = lax.all_gather(clip_id, "group", axis=1, tiled=True)
    total = ids.shape[1]
    index = jnp.arange(total, dtype=jnp.int32)[None, :]
    prev = jnp.concatenate([jnp.full_like(ids[:, :1], -1), ids[:, :-1]], axis=1)
    boundary = ids != prev
    start = lax.cummax(jnp.where(boundary, index, 0), axis=1)
    position = index - start
    ext = jnp.concatenate([jnp.full_like(ids[:, :2], -1), ids], axis=1)
    same = jnp.stack([ext[:, 2 - k : 2 - k + total] == ids for k in range(3)], axis=0)
    first = lax.axis_index("group") * frames
    pos_pad = jnp.concatenate([jnp.zeros_like(position[:, :2]), position], axis=1)
    pos_wide = lax.dynamic_slice_in_dim(pos_pad, first, frames + 2, axis=1)
    same_pad = jnp.concatenate([same, jnp.zeros_like(same[:, :, :2])], axis=2)
    own = lax.dynamic_slice_in_dim(same_pad, first, frames + 2, axis=2)
    fwd = own[:, :, :frames]
    bwd = jnp.stack([own[k, :, k : k + frames] for k in range(3)], axis=0)
    return pos_wide, fwd, bwd


def local(video, cotangent, weight, clip_id):
    frames = video.shape[1]
    rows = video.shape[2]
    cols = video.shape[3]
    chans = video.shape[4]
    past = passed_along(lax.slice_in_dim(video, frames - 2, None, axis=1), "group", 1)
    vwide = row_halo(jnp.concatenate([past, video], axis=1), "space", 2)
    pos_wide, same_fwd, same_bwd = clip_tables(clip_id, frames)
    omega = 0.37 * (jnp.arange(chans) % 8 + 1).astype(jnp.float32)
    embed = jnp.sin(pos_wide.astype(jnp.float32)[:, :, None] * omega)
    shifted = (vwide.astype(jnp.float32) + embed[:, :, None, None, :]).astype(jnp.bfloat16)
    row = jnp.arange(rows + 2)
    where_s = lax.axis_index("space")
    inside = ((row > 0) | (where_s > 0)) & ((row < rows + 1) | (where_s < lax.axis_size("space") - 1))
    shifted = jnp.where(inside[None, None, :, None, None], shifted, jnp.zeros_like(shifted))
    maskf = same_fwd.astype(jnp.float32)
    widened = jnp.pad(shifted, ((0, 0), (0, 0), (0, 0), (1, 1), (0, 0)))
    stacked = jnp.concatenate([widened[:, :, :, b : b + cols] for b in range(3)], axis=4)
    taps = weight.reshape(3, 3, 3 * chans, chans)
    pre = jnp.zeros(video.shape, jnp.float32)
    for k in range(3):
        part = jnp.zeros(video.shape, jnp.float32)
        for a in range(3):
            block = stacked[:, 2 - k : 2 - k + frames, a : a + rows]
            part = part + jnp.einsum(
                "sfhwk,kc->sfhwc", block, taps[k, a], preferred_element_type=jnp.float32
            )
        pre = pre + part * maskf[k][:, :, None, None, None]
    sigma = jax.nn.sigmoid(pre)
    activation = (pre * sigma).astype(jnp.bfloat16)
    delta = (cotangent.astype(jnp.float32) * sigma * (1.0 + pre * (1.0 - sigma))).astype(
        jnp.bfloat16
    )
    ahead = passed_along(lax.slice_in_dim(delta, 0, 2, axis=1), "group", -1)
    gwide = row_halo(jnp.concatenate([delta, ahead], axis=1), "space", 2)
    terms = []
    for k in range(3):
        masked = delta * same_fwd[k].astype(jnp.bfloat16)[:, :, None, None, None]
        for a in range(3):
            block = stacked[:, 2 - k : 2 - k + frames, a : a + rows]
            block = block.reshape(block.shape[:4] + (3, chans))
            terms.append(
                jnp.einsum("sfhwbi,sfhwc->ibc", block, masked, preferred_element_type=jnp.float32)
            )
    total = jnp.stack(terms, axis=1).reshape(chans, 27, chans)
    ng, nd, ns = lax.axis_size("group"), lax.axis_size("dp"), lax.axis_size("space")
    total = total.reshape(ng * nd, ns, 27, chans)
    if STAGED:
        where = lax.axis_index("space")
        keep = lax.dynamic_index_in_dim(total, where, axis=1, keepdims=False)
        give = lax.dynamic_index_in_dim(total, 1 - where, axis=1, keepdims=False)
        total = keep + lax.ppermute(give, "space", [(0, 1), (1, 0)])
    else:
        total = lax.psum_scatter(total, "space", scatter_dimension=1, tiled=True)
        total = total.reshape(ng * nd, 27, chans)
    total = lax.psum_scatter(total, ("group", "dp"), scatter_dimension=0, tiled=True)
    reduced = total.reshape(27, chans)
    gwide = jnp.pad(gwide, ((0, 0), (0, 0), (0, 0), (1, 1), (0, 0)))
    gstack = jnp.concatenate([gwide[:, :, :, 2 - b : 2 - b + cols] for b in range(3)], axis=4)
    back = (
        weight.reshape(3, 3, 3, chans, chans)
        .transpose(0, 1, 2, 4, 3)
        .reshape(3, 3, 3 * chans, chans)
    )
    grad = jnp.zeros(video.shape, jnp.float32)
    for k in range(3):
        part = jnp.zeros(video.shape, jnp.float32)
        for a in range(3):
            block = gstack[:, k : k + frames, 2 - a : 2 - a + rows]
            part = part + jnp.einsum(
                "sfhwk,kc->sfhwc", block, back[k, a], preferred_element_type=jnp.float32
            )
        grad = grad + part * same_bwd[k].astype(jnp.float32)[:, :, None, None, None]
    return (activation, grad.astype(jnp.bfloat16), reduced)


def solution(mesh):
    placed = (
        P("dp", "group", "space", None, None),
        P("dp", "group", "space", None, None),
        P(),
        P("dp", "group"),
    )
    return jax.shard_map(
        local,
        mesh=mesh,
        in_specs=placed,
        out_specs=(
            P("dp", "group", "space", None, None),
            P("dp", "group", "space", None, None),
            P(None, ("group", "dp", "space")),
        ),
        check_vma=False,
    )
```

time: 1460 us -> 435 us (0.30)
  the two profiles are of different devices: /device:TPU:0 before, /device:TPU:25 now
where the time goes in v1:
time: 435 us; the launch traced here: 428 us
  waiting for transfers between devices  229 us (53%)
  local copies, waits for them, and re-layouts  86.5 us (20%)
  matrix products  49.1 us (11%)
  starting transfers between devices  19.7 us (5%)
  between operations  15.1 us (3%)
  blocking collectives  14.6 us (3%)
  other arithmetic  13.8 us (3%)
    unnamed x2, waiting for transfers between devices  223 us
    another operation x9, local copies, waits for them, and re-layouts  41.2 us
    dot_general x9, matrix products, local(): jnp.einsum('sfhwbi,sfhwc->ibc', block, masked, preferred_element_type=jnp...  25.6 us
    dot_general x9, matrix products, local(): jnp.einsum('sfhwk,kc->sfhwc', block, taps[k, a], preferred_element_type=j...  17.3 us
    unnamed x1, blocking collectives  14.6 us
    unnamed x56, local copies, waits for them, and re-layouts  13.7 us
    another operation x1, local copies, waits for them, and re-layouts, local(): total = total.reshape(ng * nd, ns, 27, chans)  9.4 us
    dynamic_slice x1, local copies, waits for them, and re-layouts, local(): keep = lax.dynamic_index_in_dim(total, where, axis=1, keepdims=False)  9.19 us
  transfers between devices with their start and end apart: 8, of which 3 were waited for; matrix products, arithmetic and copies ran while one was open for 6% of the time, Pallas kernels for 0%

profile of v1, /device:TPU:25, one launch (start us, length us, event | category | flops | bytes accessed | tf_op | source)
XLA Modules:
  0.0 428.1 jit_solution(5450458517255400590)
XLA Ops:
  7.2 3.1 collective-permute-start
  10.4 1.3 dynamic-slice
  12.3 0.8 bitcast_dynamic-update-slice_fusion
  13.0 14.6 %all-reduce.5 = s32[32]{0:T(128)S(1)} all-reduce(s32[32]{0:T(128)S(1)} %bitcast_dynamic-update-slice_fusion), channel_id=1, replica_groups=mesh['group'=16,'dp'=8,'space'=2] {'group'}, use_global_device_ids=true, to_apply=%add.5 | all-reduce | flops 32 | bytes 256
  28.5 1.1 constant_dynamic-update-slice_fusion
  29.6 5.2 %collective-permute-start.2 = (bf16[1,4,1,64,256]{4,3,2,1,0:T(8,128)(2,1)S(1)}, bf16[1,4,1,64,256]{4,3,2,1,0:T(8,128)(2,1)S(1)}, u32[]{:S(2)}, u32[]{:S(2)}) collective-permute-start(bf16[1,4,1,64,256]{4,3,2,1,0:T(8,128)(2,1)S(1)} %get-tuple-element.21), channel_id=1, source_target_pairs={{1,0},{3,2},{5,4},{7,6},{9,8},{11,10},{13,12},{15,14},{17,16},{19,... | collective-permute-start | bytes 393224 | tf_op jit(solution)/shard_map/ppermute | solution.py:22
  34.8 1.3 collective-permute-start.1
  36.2 1.9 collective-permute-done.1
  38.4 0.9 pad_slice_fusion.1
  39.7 3.0 copy-done.4
  42.7 1.6 fusion.10
  44.3 1.6 fusion.12
  45.9 1.6 fusion.16
  47.5 1.6 fusion.18
  49.1 1.6 fusion.22
  50.8 1.6 fusion.24
  52.3 4.1 fusion.199
  56.4 5.3 %reshape.412 = bf16[2,8,64,3,256]{4,3,2,1,0:T(4,128)(2,1)} reshape(bf16[1,2,8,64,768]{4,3,2,1,0:T(8,128)(2,1)} %get-tuple-element.13) | data formatting | bytes 3145728 | tf_op jit(solution)/shard_map/reshape.64
  61.6 5.3 %reshape.413 = bf16[2,8,64,3,256]{4,3,2,1,0:T(4,128)(2,1)} reshape(bf16[1,2,8,64,768]{4,3,2,1,0:T(8,128)(2,1)} %get-tuple-element.12) | data formatting | bytes 3145728 | tf_op jit(solution)/shard_map/reshape.66
  66.9 5.3 %reshape.414 = bf16[2,8,64,3,256]{4,3,2,1,0:T(4,128)(2,1)} reshape(bf16[1,2,8,64,768]{4,3,2,1,0:T(8,128)(2,1)} %get-tuple-element.11) | data formatting | bytes 3145728 | tf_op jit(solution)/shard_map/reshape.68
  72.2 5.3 %reshape.416 = bf16[2,8,64,3,256]{4,3,2,1,0:T(4,128)(2,1)} reshape(bf16[1,2,8,64,768]{4,3,2,1,0:T(8,128)(2,1)} %get-tuple-element.10) | data formatting | bytes 3145728 | tf_op jit(solution)/shard_map/reshape.71
  77.5 5.3 %reshape.417 = bf16[2,8,64,3,256]{4,3,2,1,0:T(4,128)(2,1)} reshape(bf16[1,2,8,64,768]{4,3,2,1,0:T(8,128)(2,1)} %get-tuple-element.9) | data formatting | bytes 3145728 | tf_op jit(solution)/shard_map/reshape.73
  82.8 5.3 %reshape.418 = bf16[2,8,64,3,256]{4,3,2,1,0:T(4,128)(2,1)} reshape(bf16[1,2,8,64,768]{4,3,2,1,0:T(8,128)(2,1)} %get-tuple-element.8) | data formatting | bytes 3145728 | tf_op jit(solution)/shard_map/reshape.75
  88.0 5.3 %reshape.420 = bf16[2,8,64,3,256]{4,3,2,1,0:T(4,128)(2,1)} reshape(bf16[1,2,8,64,768]{4,3,2,1,0:T(8,128)(2,1)} %get-tuple-element.7) | data formatting | bytes 3145728 | tf_op jit(solution)/shard_map/reshape.78
  93.3 2.1 reshape.421
  95.4 2.2 reshape.422
  97.6 2.9 fusion.79
  101.2 1.6 fusion.70
  102.9 3.2 fusion.150
  106.2 2.9 fusion.98
  109.0 2.9 fusion.104
  111.9 2.9 fusion.110
  114.8 2.8 fusion.116
  117.6 2.8 fusion.122
  120.5 2.9 fusion.128
  123.3 2.9 fusion.134
  126.2 2.9 fusion.140
  129.1 2.7 fusion.146
  131.8 9.4 %reshape_reshape.3 = f32[128,2,27,256]{3,1,0,2:T(2,128)} reshape(f32[256,9,3,256]{3,0,2,1:T(8,128)} %fusion.146) | data formatting | bytes 14155776 | tf_op jit(solution)/shard_map/reshape;reshape | solution.py:92
  141.2 9.2 %constant_dynamic-slice_fusion.1 = (f32[128,1,27,256]{3,1,0,2:T(1,128)S(1)}, f32[128,1,27,256]{3,1,0,2:T(1,128)S(1)}) fusion(f32[128,2,27,256]{3,1,0,2:T(2,128)} %reshape_reshape.3, s32[]{:T(128)S(6)} %select_n.42, s32[]{:T(128)S(6)} %select_n.43), kind=kLoop, calls=%fused_computation.187 | loop fusion | bytes 14155784 | tf_op jit(solution)/shard_map/jit(dynamic_index_in_dim)/dynamic_slice | solution.py:95
  150.4 2.2 copy.147
  152.7 5.6 %collective-permute-start.3 = (bf16[1,2,8,64,256]{4,3,2,1,0:T(8,128)(2,1)}, bf16[1,2,8,64,256]{4,3,2,1,0:T(8,128)(2,1)}, u32[]{:S(2)}, u32[]{:S(2)}) collective-permute-start(bf16[1,2,8,64,256]{4,3,2,1,0:T(8,128)(2,1)} %get-tuple-element.33), channel_id=1, source_target_pairs={{16,0},{32,16},{48,32},{64,48},{80,64},{96,80},{112,96},{128,112},... | collective-permute-start | bytes 1572872 | tf_op jit(solution)/shard_map/ppermute | solution.py:12
  158.3 6.0 %copy.45 = bf16[3,3,3,256,256]{3,4,2,1,0:T(8,128)(2,1)} copy(bf16[3,3,3,256,256]{4,3,2,1,0:T(8,128)(2,1)} %bitcast.447) | data formatting | bytes 7077888 | tf_op jit(solution)/shard_map/reshape | solution.py:106
  164.4 0.6 dynamic-slice.1
  164.9 4.6 %collective-permute-done.3 = bf16[1,2,8,64,256]{4,3,2,1,0:T(8,128)(2,1)} collective-permute-done((bf16[1,2,8,64,256]{4,3,2,1,0:T(8,128)(2,1)}, bf16[1,2,8,64,256]{4,3,2,1,0:T(8,128)(2,1)}, u32[]{:S(2)}, u32[]{:S(2)}) %collective-permute-start.3) | collective-permute-done | bytes 524320 | tf_op jit(solution)/shard_map/ppermute | solution.py:12
  169.6 1.0 pad_maximum_fusion.3
  170.5 3.1 collective-permute-start.5
  173.6 1.3 collective-permute-start.4
  174.9 2.3 fusion.160
  177.2 0.6 copy-done.16
  177.9 3.2 select_maximum_fusion
  181.0 4.3 %bitcast_add_fusion = f32[128,27,256]{2,0,1:T(8,128)} fusion(f32[128,27,256]{2,0,1:T(8,128)} %collective-permute-done.6, f32[128,1,27,256]{3,1,0,2:T(1,128)S(1)} %get-tuple-element.3), kind=kLoop, calls=%fused_computation.5 | loop fusion | flops 884736 | bytes 10616832 | tf_op jit(solution)/shard_map/add | solution.py:97
  185.4 1.3 copy-done.2
  186.8 0.9 fusion.200
  187.7 1.6 pad_maximum_fusion.1
  189.3 0.7 copy-done.3
  191.2 0.6 fusion.4
  191.8 0.6 fusion.5
  193.6 0.6 fusion.92
  194.2 0.6 fusion.89
  194.8 1.4 fusion.149
  196.3 222.7 %all-reduce.9.cloned.1.call-done = f32[128,27,256]{2,0,1:T(8,128)} async-done(((f32[128,27,256]{2,0,1:T(8,128)}), f32[128,27,256]{2,0,1:T(8,128)}) %all-reduce.9.cloned.1.call-update) | async-done | bytes 3538960
  419.0 1.6 constant_dynamic-slice_fusion.3
  420.6 0.6 copy.148
  (75 shorter events, 5.0 us)
Async XLA Ops:
  7.2 411.8 %all-reduce.9.cloned.1.call-start = ((), (), s32[]{:S(2)}) async-start(), calls=%async_computation | async-start | bytes 7077888
  7.2 21.2 %collective-permute-start = (bf16[1,2,8,64,256]{4,3,2,1,0:T(8,128)(2,1)}, bf16[1,2,8,64,256]{4,3,2,1,0:T(8,128)(2,1)S(1)}, u32[]{:S(2)}, u32[]{:S(2)}) collective-permute-start(bf16[1,2,8,64,256]{4,3,2,1,0:T(8,128)(2,1)} %param.4), channel_id=1, source_target_pairs={{0,16},{16,32},{32,48},{48,64},{64,80},{80,96},{96,112},{112,128},... | collective-permute-start | bytes 1572872 | tf_op jit(solution)/shard_map/ppermute | solution.py:12
  29.6 6.6 %collective-permute-start.2 = (bf16[1,4,1,64,256]{4,3,2,1,0:T(8,128)(2,1)S(1)}, bf16[1,4,1,64,256]{4,3,2,1,0:T(8,128)(2,1)S(1)}, u32[]{:S(2)}, u32[]{:S(2)}) collective-permute-start(bf16[1,4,1,64,256]{4,3,2,1,0:T(8,128)(2,1)S(1)} %get-tuple-element.21), channel_id=1, source_target_pairs={{1,0},{3,2},{5,4},{7,6},{9,8},{11,10},{13,12},{15,14},{17,16},{19,... | collective-permute-start | bytes 393224 | tf_op jit(solution)/shard_map/ppermute | solution.py:22
  34.8 3.2 collective-permute-start.1
  39.3 3.4 copy-start.4
  39.7 12.6 %copy-start = (bf16[1,4,10,64,768]{4,3,2,1,0:T(8,128)(2,1)}, bf16[1,4,10,64,768]{4,3,2,1,0:T(8,128)(2,1)S(1)}, u32[]{:S(2)}) copy-start(bf16[1,4,10,64,768]{4,3,2,1,0:T(8,128)(2,1)S(1)} %pad_maximum_fusion) | copy-start | bytes 11796484
  95.4 5.1 %copy-start.15 = (f32[2,8,64,256]{3,2,1,0:T(8,128)S(1)}, f32[2,8,64,256]{3,2,1,0:T(8,128)}, u32[]{:S(2)}) copy-start(f32[2,8,64,256]{3,2,1,0:T(8,128)} %fusion.18) | copy-start | bytes 3145732
  97.6 3.3 copy-start.1
  97.6 3.6 copy-start.14
  100.5 2.4 copy-start.20
  100.5 2.4 copy-start.22
  100.5 2.4 copy-start.23
  102.9 3.2 copy-start.12
  106.2 2.9 copy-start.13
  109.0 2.9 copy-start.11
  111.9 2.9 copy-start.10
  114.8 2.9 copy-start.9
  117.6 2.8 copy-start.8
  120.5 2.9 copy-start.7
  123.3 2.9 copy-start.6
  126.2 2.9 copy-start.5
  152.6 28.5 %collective-permute-start.6 = (f32[128,27,256]{2,0,1:T(8,128)}, f32[128,27,256]{2,0,1:T(8,128)}, u32[]{:S(2)}, u32[]{:S(2)}) collective-permute-start(f32[128,27,256]{2,0,1:T(8,128)} %bitcast.432), channel_id=1, source_target_pairs={{0,1},{1,0},{2,3},{3,2},{4,5},{5,4},{6,7},{7,6},{8,9},{9,8},{10,11... | collective-permute-start | bytes 10616840 | tf_op jit(solution)/shard_map/ppermute | solution.py:97
  152.7 16.8 %collective-permute-start.3 = (bf16[1,2,8,64,256]{4,3,2,1,0:T(8,128)(2,1)}, bf16[1,2,8,64,256]{4,3,2,1,0:T(8,128)(2,1)}, u32[]{:S(2)}, u32[]{:S(2)}) collective-permute-start(bf16[1,2,8,64,256]{4,3,2,1,0:T(8,128)(2,1)} %get-tuple-element.33), channel_id=1, source_target_pairs={{16,0},{32,16},{48,32},{64,48},{80,64},{96,80},{112,96},{128,112},... | collective-permute-start | bytes 1572872 | tf_op jit(solution)/shard_map/ppermute | solution.py:12
  158.3 6.0 %copy-start.21 = (u32[256]{0:T(256)S(1)}, u32[256]{0:T(256)}, u32[]{:S(2)}) copy-start(u32[256]{0:T(256)} %constant.84) | copy-start | bytes 3076
  170.5 6.7 %collective-permute-start.5 = (bf16[1,4,1,64,256]{4,3,2,1,0:T(8,128)(2,1)S(1)}, bf16[1,4,1,64,256]{4,3,2,1,0:T(8,128)(2,1)S(1)}, u32[]{:S(2)}, u32[]{:S(2)}) collective-permute-start(bf16[1,4,1,64,256]{4,3,2,1,0:T(8,128)(2,1)S(1)} %get-tuple-element.19), channel_id=1, source_target_pairs={{1,0},{3,2},{5,4},{7,6},{9,8},{11,10},{13,12},{15,14},{17,16},{19,... | collective-permute-start | bytes 393224 | tf_op jit(solution)/shard_map/ppermute | solution.py:22
  173.6 3.6 collective-permute-start.4
  177.2 0.7 copy-start.16
  177.9 3.2 copy-start.18
  185.4 1.4 copy-start.2
  186.8 0.9 copy-start.17
  186.8 1.0 copy-start.19
  187.7 2.3 copy-start.3
Sparse Core Ops, SparseCore 0:
  185.5 233.4 all-reduce.8
